TPU v7x, 32 devices: a whole 2x2x4 slice. The times are simulated.
32 devices in a mesh: dom: 4 (over x, core), fsdp: 8 (over z, y).
Axes of the slice: x: 2, y: 2, z: 4, core: 2. Of those that a mesh axis runs over, the one named last changes fastest.
Arguments:
- acts: bfloat16 [4096, 14336], P(('dom', 'fsdp')), may hold values from -24 to 24
- cotangent: bfloat16 [4096, 4096], P(('dom', 'fsdp')), may hold values from -0.75 to 0.75
- weight: bfloat16 [14336, 4096], P(('dom', 'fsdp')), may hold values from -0.046875 to 0.046875
- moment: float32 [14336, 4096], P(('dom', 'fsdp')), may hold values from -6 to 6
- second: float32 [14336, 4096], P(('dom', 'fsdp')), may hold values from 0.3 to 3
- log_weights: float32 [4], replicated, may hold values from -1 to 1
- domain_ids: int32 [4], replicated, may hold values from 0 to 3, each once
- step_count: int32 [1], replicated, may hold values from 1 to 8
Outputs:
- new_weight: bfloat16 [14336, 4096], P(('dom', 'fsdp'))
- new_moment: float32 [14336, 4096], P(('dom', 'fsdp'))
- new_second: float32 [14336, 4096], P(('dom', 'fsdp'))
- new_domain_weights: float32 [4], replicated
All inputs are finite; a program needn't handle non-finite values.
Results may differ from a plain program's by a relative error of at most 0.001.
Values may be sent and summed in bfloat16 or wider, within the bound.
No kernel may reach another device: no remote copies, remote signals or barrier semaphores. Data moves between devices by JAX's collectives and lax.ppermute only.
A program may use at most 192 MiB of HBM per device.

v0:
```python
import jax
import jax.numpy as jnp
from jax import lax
from jax.sharding import Mesh, PartitionSpec as P

FLAT = ("x", "core", "fsdp")


def on_device(acts, cotangent, weight, moment, second, log_weights, domain_ids, step_count):
    groups = lax.axis_size("x") * lax.axis_size("core")
    devices = lax.axis_size(FLAT)
    tok_rows = acts.shape[0]
    group_tok = devices // groups * tok_rows
    width = cotangent.shape[1]
    own_rows = weight.shape[0]
    core = lax.axis_index("core")
    shaped = acts.reshape(tok_rows, devices, own_rows)
    columns = lax.all_to_all(shaped, FLAT, split_axis=1, concat_axis=0, tiled=True)
    columns = columns.reshape(groups, group_tok, own_rows)
    mine = lax.all_gather(cotangent, ("x", "fsdp"), axis=0, tiled=True)
    mine = mine.reshape(groups // 2, group_tok, width)
    theirs = lax.ppermute(mine, "core", [(0, 1), (1, 0)])
    half = jnp.arange(groups // 2, dtype=jnp.int32) * 2
    order = jnp.concatenate([half + core, half + 1 - core])
    local_cols = jnp.take(columns, order, axis=0)
    dims = (((1,), (1,)), ((0,), (0,)))
    g_mine = lax.dot_general(
        local_cols[: groups // 2], mine, dims, preferred_element_type=jnp.float32
    )
    g_theirs = lax.dot_general(
        local_cols[groups // 2 :], theirs, dims, preferred_element_type=jnp.float32
    )
    owned = jnp.concatenate([g_mine, g_theirs]).astype(jnp.bfloat16)
    pairs = {}
    for i in range(groups):
        for j in range(i, groups):
            pairs[i, j] = jnp.sum(owned[i].astype(jnp.float32) * owned[j].astype(jnp.float32))
    local_gram = jnp.stack(
        [jnp.stack([pairs[min(i, j), max(i, j)] for j in range(groups)]) for i in range(groups)]
    )
    perm = (order[:, None] == jnp.arange(groups, dtype=jnp.int32)[None, :]).astype(jnp.float32)
    device_gram = jnp.dot(
        perm.T,
        jnp.dot(local_gram, perm, precision=lax.Precision.HIGHEST),
        precision=lax.Precision.HIGHEST,
    )
    gram = lax.psum(device_gram, FLAT)
    score = jnp.sum(gram, axis=1) * (groups / jnp.trace(gram))
    onehot = (domain_ids[:, None] == jnp.arange(groups, dtype=jnp.int32)[None, :]).astype(
        jnp.float32
    )
    logits = log_weights + 2.0 * jnp.sum(onehot * score[:, None], axis=0)
    new_domain_weights = jax.nn.softmax(logits)
    group_w = jnp.sum(onehot * new_domain_weights[None, :], axis=1)
    local_w = jnp.take(group_w, order)
    combined = jnp.zeros((own_rows, width), jnp.float32)
    for group in range(groups):
        combined = combined + local_w[group] * owned[group].astype(jnp.float32)
    steps_f = step_count[0].astype(jnp.float32)
    new_moment = 0.9 * moment + 0.1 * combined
    new_second = 0.95 * second + 0.05 * combined * combined
    fix_one = 1.0 - jnp.exp(steps_f * jnp.log(jnp.float32(0.9)))
    fix_two = 1.0 - jnp.exp(steps_f * jnp.log(jnp.float32(0.95)))
    update = new_moment / fix_one / (jnp.sqrt(new_second / fix_two) + 1e-08)
    new_weight = (weight.astype(jnp.float32) - 0.002 * update).astype(jnp.bfloat16)
    return (new_weight, new_moment, new_second, new_domain_weights)


def solution(mesh):
    chips = mesh.shape["dom"] // 2
    flat = Mesh(mesh.devices.reshape(chips, 2, mesh.shape["fsdp"]), FLAT)
    row = P(FLAT, None)
    return jax.shard_map(
        on_device,
        mesh=flat,
        in_specs=(row, row, row, row, row, P(), P(), P()),
        out_specs=(row, row, row, P()),
        check_vma=False,
    )
```

profile of v0, /device:TPU:10, one launch (start us, length us, event | category | flops | bytes accessed | tf_op | source)
XLA Modules:
  0.0 442.7 jit_solution(5612027827097999883)
XLA Ops:
  7.2 0.0 all-gather.2.cloned.1.call-start
  7.2 0.7 all-gather.2.cloned.1.call-update
  7.9 193.8 %all-gather.2.cloned.1.call-done = bf16[2048,4096]{1,0:T(8,128)(2,1)} async-done(((bf16[128,4096]{1,0:T(8,128)(2,1)}), bf16[2048,4096]{1,0:T(8,128)(2,1)}) %all-gather.2.cloned.1.call-update) | async-done | bytes 16777232 | tf_op jit(solution)/shard_map/all_gather | solution.py:20
  201.7 0.0 collective-permute-start
  201.7 6.0 %copy.12 = bf16[128,14336]{0,1:T(8,128)(2,1)} copy(bf16[128,14336]{1,0:T(8,128)(2,1)} %param.8) | data formatting | bytes 7340032 | tf_op args[0]
  207.8 5.6 %all-to-all-start = ((bf16[128,32,448]{0,2,1:T(8,128)(2,1)}), bf16[128,32,448]{0,2,1:T(8,128)(2,1)}, u32[]{:S(2)}, u32[]{:S(2)}) async-start(bf16[128,32,448]{0,2,1:T(8,128)(2,1)} %bitcast.50), calls=%async_computation | async-start | bytes 7340032 | tf_op jit(solution)/shard_map/all_to_all | solution.py:18
  214.1 0.1 fusion.26
  214.2 0.1 compare_and_fusion
  214.2 79.3 %all-to-all-done = bf16[128,32,448]{0,2,1:T(8,128)(2,1)} async-done(((bf16[128,32,448]{0,2,1:T(8,128)(2,1)}), bf16[128,32,448]{0,2,1:T(8,128)(2,1)}, u32[]{:S(2)}, u32[]{:S(2)}) %all-to-all-start) | async-done | bytes 3670048 | tf_op jit(solution)/shard_map/all_to_all | solution.py:18
  293.6 6.2 %copy.13 = bf16[32,128,1,448]{1,0,3,2:T(8,128)(2,1)} copy(bf16[32,128,1,448]{1,3,0,2:T(8,128)(2,1)} %bitcast.2) | data formatting | bytes 7340032 | tf_op jit(solution)/shard_map/all_to_all | solution.py:18
  299.8 6.3 %reshape.125 = bf16[4,1024,448]{1,0,2:T(4,128)(2,1)} reshape(bf16[32,128,1,448]{1,0,3,2:T(8,128)(2,1)} %copy.13) | data formatting | bytes 7340032 | tf_op jit(solution)/shard_map/reshape | solution.py:19
  306.1 5.1 %copy.14 = bf16[4,1024,448]{1,2,0:T(8,128)(2,1)} copy(bf16[4,1024,448]{1,0,2:T(4,128)(2,1)} %reshape.125) | data formatting | bytes 7340032 | tf_op jit(solution)/shard_map/reshape | solution.py:19
  311.2 4.7 %gather_fusion = bf16[4,1024,448]{1,2,0:T(8,128)(2,1)} fusion(bf16[4,1024,448]{1,2,0:T(8,128)(2,1)} %copy.14, s32[1024]{0:T(1024)S(1)} %pad_clamp_fusion), kind=kCustom, calls=%fused_computation | custom fusion | bytes 7340048 | tf_op jit(solution)/shard_map/jit(_take)/gather | solution.py:25
  315.8 13.8 %convolution_convert_fusion.1 = bf16[2,448,4096]{2,1,0:T(8,128)(2,1)} fusion(bf16[2,1024,4096]{2,1,0:T(8,128)(2,1)} %bitcast.52, bf16[4,1024,448]{1,2,0:T(8,128)(2,1)} %gather_fusion, pred[4]{0:T(512)(128)(4,1)S(1)} %get-tuple-element.21), kind=kOutput, calls=%fused_computation.35 | convolution fusion | flops 7521697792 | bytes 27787268 | tf_op jit(solution)/shard_map/dot_general | solution.py:27
  329.6 0.0 collective-permute-done
  329.6 14.0 %convolution_convert_fusion = bf16[2,448,4096]{2,1,0:T(8,128)(2,1)} fusion(bf16[2,1024,4096]{2,1,0:T(8,128)(2,1)} %collective-permute-done, bf16[4,1024,448]{1,2,0:T(8,128)(2,1)} %gather_fusion, pred[4]{0:T(512)(128)(4,1)S(1)} %get-tuple-element.21), kind=kOutput, calls=%fused_computation.34 | convolution fusion | flops 7521697792 | bytes 27787268 | tf_op jit(solution)/shard_map/dot_general | solution.py:30
  343.6 0.0 copy-start.1
  343.6 0.0 copy-start
  343.6 9.2 %fusion.8 = (f32[]{:T(128)}, f32[]{:T(128)}, f32[]{:T(128)}, f32[]{:T(128)}, f32[]{:T(128)}, /*index=5*/f32[]{:T(128)}, f32[]{:T(128)}, f32[]{:T(128)}, f32[]{:T(128)}, f32[]{:T(128)}) fusion(bf16[2,448,4096]{2,1,0:T(8,128)(2,1)} %convolution_convert_fusion, bf16[2,448,4096]{2,1,0:T(8,128)(2,1)} %convolution_convert_fusion.1), kind=kLoop, calls=%fused_computation.25 | loop fusion | flops 44040188 | bytes 14680104 | tf_op jit(solution)/shard_map/reduce_sum | solution.py:37
  352.7 2.6 maximum_bitcast_fusion
  355.3 2.6 maximum_bitcast_fusion.1
  357.9 2.7 maximum_bitcast_fusion.2
  360.6 2.7 maximum_bitcast_fusion.3
  363.3 0.2 fusion.15
  363.5 0.3 fusion.23
  363.7 43.1 %psum.7 = f32[4,4]{1,0:T(4,128)S(1)} all-reduce(f32[4,4]{1,0:T(4,128)S(1)} %fusion.23), channel_id=1, replica_groups=mesh['x'=2,'core'=2,'fsdp'=8] {'x','core','fsdp'}, use_global_device_ids=true, to_apply=%region_10.11 | all-reduce | flops 16 | bytes 128 | tf_op jit(solution)/shard_map/psum | solution.py:47
  406.8 0.6 select_reduce_fusion.2
  408.2 0.0 copy-done.1
  408.2 0.1 select_reduce_fusion.1
  408.3 0.0 copy-done
  408.3 0.6 fusion.31
  408.9 1.3 fusion.35
  410.1 0.6 broadcast_divide_fusion
  410.8 0.0 copy-start.2
  410.8 0.2 select_reduce_fusion
  411.0 0.6 gather_fusion.1
  411.6 0.7 fusion.36
  412.3 23.5 %subtract_convert_fusion = (bf16[448,4096]{1,0:T(8,128)(2,1)}, f32[448,4096]{1,0:T(8,128)}, f32[448,4096]{1,0:T(8,128)}) fusion(bf16[448,4096]{1,0:T(8,128)(2,1)} %param.10, f32[]{:T(128)} %bitcast.27, f32[]{:T(128)} %bitcast.26, bf16[2,448,4096]{2,1,0:T(8,128)(2,1)} %convolution_convert_fusion, f32[]{:T(128)} %bitcast.24, f32[]{:T(128)} %bitcast.23, ...), kind=kLoop, calls=%fused_computation.32 | loop fusion | flops 47710208 | bytes 51380248 | tf_op jit(solution)/shard_map/convert_element_type | solution.py:65
  435.8 0.0 copy-done.2
  (5 shorter events, 0.0 us)
Async XLA Ops:
  7.2 194.5 %all-gather.2.cloned.1.call-start = ((), (), s32[]{:S(2)}) async-start(), calls=%async_computation.1 | async-start | bytes 17825792 | tf_op jit(solution)/shard_map/all_gather | solution.py:20
  201.7 127.9 %collective-permute-start = (bf16[2,1024,4096]{2,1,0:T(8,128)(2,1)}, bf16[2,1024,4096]{2,1,0:T(8,128)(2,1)}, u32[]{:S(2)}, u32[]{:S(2)}) collective-permute-start(bf16[2,1024,4096]{2,1,0:T(8,128)(2,1)} %bitcast.51), channel_id=1, source_target_pairs={{0,8},{8,0},{1,9},{9,1},{2,10},{10,2},{3,11},{11,3},{4,12},{12,4},... | collective-permute-start | bytes 50331656 | tf_op jit(solution)/shard_map/ppermute | solution.py:22
  207.8 85.8 %all-to-all-start = ((bf16[128,32,448]{0,2,1:T(8,128)(2,1)}), bf16[128,32,448]{0,2,1:T(8,128)(2,1)}, u32[]{:S(2)}, u32[]{:S(2)}) async-start(bf16[128,32,448]{0,2,1:T(8,128)(2,1)} %bitcast.50), calls=%async_computation | async-start | bytes 7340032 | tf_op jit(solution)/shard_map/all_to_all | solution.py:18
  343.6 64.6 %copy-start.1 = (s32[4]{0:T(128)S(1)}, s32[4]{0:T(128)}, u32[]{:S(2)}) copy-start(s32[4]{0:T(128)} %param.14) | copy-start | bytes 52
  343.6 64.7 %copy-start = (f32[4]{0:T(128)S(1)}, f32[4]{0:T(128)}, u32[]{:S(2)}) copy-start(f32[4]{0:T(128)} %param.13) | copy-start | bytes 52
  410.8 25.0 %copy-start.2 = (f32[4]{0:T(128)}, f32[4]{0:T(128)S(1)}, u32[]{:S(2)}) copy-start(f32[4]{0:T(128)S(1)} %broadcast_divide_fusion) | copy-start | bytes 52
Sparse Core Ops, SparseCore 0:
  10.8 190.8 all-gather.1
where the time goes:
time: 444 us; the launch traced here: 443 us
  waiting for transfers between devices  274 us (62%)
  other arithmetic  46.9 us (11%)
  blocking collectives  43.1 us (10%)
  local copies, waits for them, and re-layouts  29.6 us (7%)
  matrix products  28.2 us (6%)
  between operations  15.5 us (3%)
  starting transfers between devices  5.61 us (1%)
    all_gather x1, waiting for transfers between devices, on_device(): mine = lax.all_gather(cotangent, ('x', 'fsdp'), axis=0, tiled=True)  194 us
    all_to_all x1, waiting for transfers between devices, on_device(): lax.all_to_all(shaped, FLAT, split_axis=1, concat_axis=0, tiled=True)  79.3 us
    psum x1, blocking collectives, on_device(): gram = lax.psum(device_gram, FLAT)  43.1 us
    convert_element_type x1, other arithmetic, on_device(): (weight.astype(jnp.float32) - 0.002 * update).astype(jnp.bfloat16)  23.5 us
    dot_general x1, matrix products, on_device(): lax.dot_general(local_cols[groups // 2:], theirs, dims, preferred_element...  14 us
    dot_general x1, matrix products, on_device(): lax.dot_general(local_cols[:groups // 2], mine, dims, preferred_element_t...  13.8 us
    reshape x2, local copies, waits for them, and re-layouts, on_device(): columns = columns.reshape(groups, group_tok, own_rows)  11.3 us
    another operation x4, other arithmetic, on_device(): jnp.stack([jnp.stack([pairs[min(i, j), max(i, j)] for j in range(groups)]...  10.6 us
  transfers between devices with their start and end apart: 3, of which 2 were waited for; matrix products, arithmetic and copies ran while one was open for 10% of the time, Pallas kernels for 0%

commit v1 on v0

--- a/solution.py
+++ b/solution.py
@@ -44,7 +44,8 @@
         jnp.dot(local_gram, perm, precision=lax.Precision.HIGHEST),
         precision=lax.Precision.HIGHEST,
     )
-    gram = lax.psum(device_gram, FLAT)
+    blocks = lax.all_gather(device_gram, FLAT, axis=0, tiled=False)
+    gram = blocks.sum(axis=0)
     score = jnp.sum(gram, axis=1) * (groups / jnp.trace(gram))
     onehot = (domain_ids[:, None] == jnp.arange(groups, dtype=jnp.int32)[None, :]).astype(
         jnp.float32

time: 444 us -> 470 us (1.059)
  blocking collectives: 43.1 us -> 64.6 us
    all_gather x0 -> x1, blocking collectives: none -> 64.6 us  [on_device(): blocks = lax.all_gather(device_gram, FLAT, axis=0, tiled=False)]
    psum x1 -> x0, blocking collectives: 43.1 us -> none  [on_device(): gram = lax.psum(device_gram, FLAT)]
  transfers between devices with their start and end apart: 3 -> 3, of which waited for: 2 -> 2; matrix products, arithmetic and copies ran while one was open for 10% -> 9% of each run, Pallas kernels for 0% -> 0%
where the time goes in v1:
time: 470 us; the launch traced here: 464 us
  waiting for transfers between devices  274 us (58%)
  blocking collectives  64.6 us (14%)
  other arithmetic  46.9 us (10%)
  local copies, waits for them, and re-layouts  29.6 us (6%)
  matrix products  28.2 us (6%)
  between operations  15.5 us (3%)
  starting transfers between devices  5.61 us (1%)
    all_gather x1, waiting for transfers between devices, on_device(): mine = lax.all_gather(cotangent, ('x', 'fsdp'), axis=0, tiled=True)  194 us
    all_to_all x1, waiting for transfers between devices, on_device(): lax.all_to_all(shaped, FLAT, split_axis=1, concat_axis=0, tiled=True)  79.3 us
    all_gather x1, blocking collectives, on_device(): blocks = lax.all_gather(device_gram, FLAT, axis=0, tiled=False)  64.6 us
    convert_element_type x1, other arithmetic, on_device(): (weight.astype(jnp.float32) - 0.002 * update).astype(jnp.bfloat16)  23.5 us
    dot_general x1, matrix products, on_device(): lax.dot_general(local_cols[groups // 2:], theirs, dims, preferred_element...  14 us
    dot_general x1, matrix products, on_device(): lax.dot_general(local_cols[:groups // 2], mine, dims, preferred_element_t...  13.8 us
    reshape x2, local copies, waits for them, and re-layouts, on_device(): columns = columns.reshape(groups, group_tok, own_rows)  11.3 us
    another operation x4, other arithmetic, on_device(): jnp.stack([jnp.stack([pairs[min(i, j), max(i, j)] for j in range(groups)]...  10.6 us
  transfers between devices with their start and end apart: 3, of which 2 were waited for; matrix products, arithmetic and copies ran while one was open for 9% of the time, Pallas kernels for 0%

profile of v1, /device:TPU:10, one launch (start us, length us, event | category | flops | bytes accessed | tf_op | source)
XLA Modules:
  0.0 464.2 jit_solution(9218684040570246565)
XLA Ops:
  7.2 0.0 all-gather.4.cloned.1.call-start
  7.2 0.7 all-gather.4.cloned.1.call-update
  7.9 193.8 %all-gather.4.cloned.1.call-done = bf16[2048,4096]{1,0:T(8,128)(2,1)} async-done(((bf16[128,4096]{1,0:T(8,128)(2,1)}), bf16[2048,4096]{1,0:T(8,128)(2,1)}) %all-gather.4.cloned.1.call-update) | async-done | bytes 16777232 | tf_op jit(solution)/shard_map/all_gather | solution.py:20
  201.7 0.0 collective-permute-start
  201.7 6.0 %copy.18 = bf16[128,14336]{0,1:T(8,128)(2,1)} copy(bf16[128,14336]{1,0:T(8,128)(2,1)} %param.8) | data formatting | bytes 7340032 | tf_op args[0]
  207.8 5.6 %all-to-all-start = ((bf16[128,32,448]{0,2,1:T(8,128)(2,1)}), bf16[128,32,448]{0,2,1:T(8,128)(2,1)}, u32[]{:S(2)}, u32[]{:S(2)}) async-start(bf16[128,32,448]{0,2,1:T(8,128)(2,1)} %bitcast.52), calls=%async_computation | async-start | bytes 7340032 | tf_op jit(solution)/shard_map/all_to_all | solution.py:18
  214.1 0.1 fusion.25
  214.2 0.1 compare_and_fusion
  214.2 79.3 %all-to-all-done = bf16[128,32,448]{0,2,1:T(8,128)(2,1)} async-done(((bf16[128,32,448]{0,2,1:T(8,128)(2,1)}), bf16[128,32,448]{0,2,1:T(8,128)(2,1)}, u32[]{:S(2)}, u32[]{:S(2)}) %all-to-all-start) | async-done | bytes 3670048 | tf_op jit(solution)/shard_map/all_to_all | solution.py:18
  293.6 6.2 %copy.19 = bf16[32,128,1,448]{1,0,3,2:T(8,128)(2,1)} copy(bf16[32,128,1,448]{1,3,0,2:T(8,128)(2,1)} %bitcast.2) | data formatting | bytes 7340032 | tf_op jit(solution)/shard_map/all_to_all | solution.py:18
  299.8 6.3 %reshape.125 = bf16[4,1024,448]{1,0,2:T(4,128)(2,1)} reshape(bf16[32,128,1,448]{1,0,3,2:T(8,128)(2,1)} %copy.19) | data formatting | bytes 7340032 | tf_op jit(solution)/shard_map/reshape | solution.py:19
  306.1 5.1 %copy.20 = bf16[4,1024,448]{1,2,0:T(8,128)(2,1)} copy(bf16[4,1024,448]{1,0,2:T(4,128)(2,1)} %reshape.125) | data formatting | bytes 7340032 | tf_op jit(solution)/shard_map/reshape | solution.py:19
  311.2 4.7 %gather_fusion = bf16[4,1024,448]{1,2,0:T(8,128)(2,1)} fusion(bf16[4,1024,448]{1,2,0:T(8,128)(2,1)} %copy.20, s32[1024]{0:T(1024)S(1)} %pad_clamp_fusion), kind=kCustom, calls=%fused_computation | custom fusion | bytes 7340048 | tf_op jit(solution)/shard_map/jit(_take)/gather | solution.py:25
  315.8 13.8 %convolution_convert_fusion.1 = bf16[2,448,4096]{2,1,0:T(8,128)(2,1)} fusion(bf16[2,1024,4096]{2,1,0:T(8,128)(2,1)} %bitcast.54, bf16[4,1024,448]{1,2,0:T(8,128)(2,1)} %gather_fusion, pred[4]{0:T(512)(128)(4,1)S(1)} %get-tuple-element.21), kind=kOutput, calls=%fused_computation.35 | convolution fusion | flops 7521697792 | bytes 27787268 | tf_op jit(solution)/shard_map/dot_general | solution.py:27
  329.6 0.0 collective-permute-done
  329.6 14.0 %convolution_convert_fusion = bf16[2,448,4096]{2,1,0:T(8,128)(2,1)} fusion(bf16[2,1024,4096]{2,1,0:T(8,128)(2,1)} %collective-permute-done, bf16[4,1024,448]{1,2,0:T(8,128)(2,1)} %gather_fusion, pred[4]{0:T(512)(128)(4,1)S(1)} %get-tuple-element.21), kind=kOutput, calls=%fused_computation.34 | convolution fusion | flops 7521697792 | bytes 27787268 | tf_op jit(solution)/shard_map/dot_general | solution.py:30
  343.6 0.0 copy-start.1
  343.6 0.0 copy-start
  343.6 9.2 %fusion.8 = (f32[]{:T(128)}, f32[]{:T(128)}, f32[]{:T(128)}, f32[]{:T(128)}, f32[]{:T(128)}, /*index=5*/f32[]{:T(128)}, f32[]{:T(128)}, f32[]{:T(128)}, f32[]{:T(128)}, f32[]{:T(128)}) fusion(bf16[2,448,4096]{2,1,0:T(8,128)(2,1)} %convolution_convert_fusion, bf16[2,448,4096]{2,1,0:T(8,128)(2,1)} %convolution_convert_fusion.1), kind=kLoop, calls=%fused_computation.25 | loop fusion | flops 44040188 | bytes 14680104 | tf_op jit(solution)/shard_map/reduce_sum | solution.py:37
  352.7 2.6 maximum_bitcast_fusion
  355.3 2.6 maximum_bitcast_fusion.1
  357.9 2.7 maximum_bitcast_fusion.2
  360.6 2.7 maximum_bitcast_fusion.3
  363.3 0.2 fusion.15
  363.5 0.3 convolution_bitcast_fusion
  363.7 64.6 %all-gather.1 = f32[32,4,4]{2,1,0:T(4,128)S(1)} all-gather(f32[1,4,4]{2,1,0:T(4,128)S(1)} %convolution_bitcast_fusion), channel_id=2, replica_groups=mesh['x'=2,'core'=2,'fsdp'=8] {'x','core','fsdp'}, dimensions={0}, use_global_device_ids=true | all-gather | bytes 2112 | tf_op jit(solution)/shard_map/all_gather | solution.py:47
  428.3 0.1 fusion.33
  428.5 0.6 select_reduce_fusion.2
  429.8 0.0 copy-done.1
  429.8 0.1 select_reduce_fusion.1
  429.9 0.0 copy-done
  429.9 0.6 fusion.30
  430.5 1.3 fusion.35
  431.7 0.6 broadcast_divide_fusion
  432.4 0.0 copy-start.2
  432.4 0.2 select_reduce_fusion
  432.6 0.6 gather_fusion.1
  433.2 0.7 fusion.36
  433.9 23.5 %subtract_convert_fusion = (bf16[448,4096]{1,0:T(8,128)(2,1)}, f32[448,4096]{1,0:T(8,128)}, f32[448,4096]{1,0:T(8,128)}) fusion(bf16[448,4096]{1,0:T(8,128)(2,1)} %param.10, f32[]{:T(128)} %bitcast.28, f32[]{:T(128)} %bitcast.27, bf16[2,448,4096]{2,1,0:T(8,128)(2,1)} %convolution_convert_fusion, f32[]{:T(128)} %bitcast.25, f32[]{:T(128)} %bitcast.24, ...), kind=kLoop, calls=%fused_computation.32 | loop fusion | flops 47710208 | bytes 51380248 | tf_op jit(solution)/shard_map/convert_element_type | solution.py:66
  457.4 0.0 copy-done.2
  (5 shorter events, 0.0 us)
Async XLA Ops:
  7.2 194.5 %all-gather.4.cloned.1.call-start = ((), (), s32[]{:S(2)}) async-start(), calls=%async_computation.1 | async-start | bytes 17825792 | tf_op jit(solution)/shard_map/all_gather | solution.py:20
  201.7 127.9 %collective-permute-start = (bf16[2,1024,4096]{2,1,0:T(8,128)(2,1)}, bf16[2,1024,4096]{2,1,0:T(8,128)(2,1)}, u32[]{:S(2)}, u32[]{:S(2)}) collective-permute-start(bf16[2,1024,4096]{2,1,0:T(8,128)(2,1)} %bitcast.53), channel_id=1, source_target_pairs={{0,8},{8,0},{1,9},{9,1},{2,10},{10,2},{3,11},{11,3},{4,12},{12,4},... | collective-permute-start | bytes 50331656 | tf_op jit(solution)/shard_map/ppermute | solution.py:22
  207.8 85.8 %all-to-all-start = ((bf16[128,32,448]{0,2,1:T(8,128)(2,1)}), bf16[128,32,448]{0,2,1:T(8,128)(2,1)}, u32[]{:S(2)}, u32[]{:S(2)}) async-start(bf16[128,32,448]{0,2,1:T(8,128)(2,1)} %bitcast.52), calls=%async_computation | async-start | bytes 7340032 | tf_op jit(solution)/shard_map/all_to_all | solution.py:18
  343.6 86.2 %copy-start.1 = (s32[4]{0:T(128)S(1)}, s32[4]{0:T(128)}, u32[]{:S(2)}) copy-start(s32[4]{0:T(128)} %param.14) | copy-start | bytes 52
  343.6 86.3 %copy-start = (f32[4]{0:T(128)S(1)}, f32[4]{0:T(128)}, u32[]{:S(2)}) copy-start(f32[4]{0:T(128)} %param.13) | copy-start | bytes 52
  432.4 25.0 %copy-start.2 = (f32[4]{0:T(128)}, f32[4]{0:T(128)S(1)}, u32[]{:S(2)}) copy-start(f32[4]{0:T(128)S(1)} %broadcast_divide_fusion) | copy-start | bytes 52
Sparse Core Ops, SparseCore 0:
  10.8 190.8 all-gather.3
